TPU v7x, 32 devices: a whole 2x2x4 slice. The times are simulated.
32 devices in a mesh: dp: 8 (over y, x, core), tensor: 4 (over z).
Axes of the slice: x: 2, y: 2, z: 4, core: 2. Of those that a mesh axis runs over, the one named last changes fastest.
Arguments:
- glu_input: bfloat16 [16, 256, 3072], P('dp', 'tensor'), may hold values from -12 to 12
- depth_kernel: float32 [31, 1536], replicated, may hold values from -1 to 1
- norm_scale: float32 [1536], replicated, may hold values from 0.5 to 1.5
- norm_shift: float32 [1536], replicated, may hold values from -3 to 3
- proj_weight: bfloat16 [1536, 1536], P('tensor'), may hold values from -0.15625 to 0.15625
- out_grad: bfloat16 [16, 256, 1536], P('dp', 'tensor'), may hold values from -6 to 6
Outputs:
- conv_output: bfloat16 [16, 256, 1536], P('dp', 'tensor')
- input_grad: bfloat16 [16, 256, 3072], P('dp', 'tensor')
- weight_grad: float32 [1536, 1536], P('tensor')
- kernel_grad: float32 [31, 1536], replicated
- scale_grad: float32 [1536], replicated
- shift_grad: float32 [1536], replicated
All inputs are finite; a program needn't handle non-finite values.
Results may differ from a plain program's by a relative error of at most 0.0057.
Values may be sent and summed in bfloat16 or wider, within the bound.
No kernel may reach another device: no remote copies, remote signals or barrier semaphores. Data moves between devices by JAX's collectives and lax.ppermute only.
A program may use at most 128 MiB of HBM per device.

v0:
```python
import jax
import jax.numpy as jnp
from jax import lax
from jax.sharding import PartitionSpec as P

epsilon = 1e-05


def extended(array, sides, width):
    for axis, dim in sides:
        peers, length = (lax.axis_size(axis), array.shape[dim])
        up = [(i, (i + 1) % peers) for i in range(peers - 1)]
        down = [(j, i) for i, j in up]
        last = lax.slice_in_dim(array, length - width, length, axis=dim)
        leading = lax.slice_in_dim(array, 0, width, axis=dim)
        before = lax.ppermute(last, axis, up)
        after = lax.ppermute(leading, axis, down)
        array = jnp.concatenate([before, array, after], axis=dim)
    return array


def is_power_of_two(n):
    return n > 0 and n & n - 1 == 0


def all_sum(x, axes):
    for axis in axes:
        peers = lax.axis_size(axis)
        if not is_power_of_two(peers):
            x = lax.psum(x, axis)
            continue
        step = 1
        while step < peers:
            x = x + lax.ppermute(x, axis, [(i, i ^ step) for i in range(peers)])
            step *= 2
    return x


def all_moments(mean, spread, count, axes):
    for axis in axes:
        peers = lax.axis_size(axis)
        step = 1
        while step < peers:
            other = lax.ppermute(
                jnp.stack([mean, spread]), axis, [(i, i ^ step) for i in range(peers)]
            )
            delta = other[0] - mean
            mean = (mean + other[0]) * 0.5
            spread = spread + other[1] + delta * delta * (count * 0.5)
            count = count * 2
            step *= 2
    return (mean, spread)


def rows_sum(x, axis):
    peers = lax.axis_size(axis)
    if not is_power_of_two(peers) or x.shape[0] % peers:
        return lax.psum(x, axis)
    me = lax.axis_index(axis)
    bits = []
    step = 1
    while step < peers:
        bit = lax.rem(me // step, 2)
        half = x.shape[0] // 2
        keep = lax.dynamic_slice_in_dim(x, bit * half, half, axis=0)
        give = lax.dynamic_slice_in_dim(x, (1 - bit) * half, half, axis=0)
        x = keep + lax.ppermute(give, axis, [(i, i ^ step) for i in range(peers)])
        bits.append((step, bit))
        step *= 2
    for step, bit in reversed(bits):
        other = lax.ppermute(x, axis, [(i, i ^ step) for i in range(peers)])
        x = jnp.where(bit == 0, jnp.concatenate([x, other]), jnp.concatenate([other, x]))
    return x


def gather_weight(block):
    if lax.axis_size("dp") % 2:
        return lax.all_gather(block, "tensor", axis=0, tiled=True)
    peers = lax.axis_size("tensor")
    half = block.shape[0] // 2
    core = lax.rem(lax.axis_index("dp"), 2)
    mine = lax.dynamic_slice_in_dim(block, core * half, half, axis=0)
    held = lax.all_gather(mine, "tensor", axis=0, tiled=False)
    other = lax.ppermute(held, "dp", [(i, i ^ 1) for i in range(lax.axis_size("dp"))])
    first = jnp.where(core == 0, held, other)
    second = jnp.where(core == 0, other, held)
    return jnp.concatenate([first, second], axis=1).reshape(peers * block.shape[0], block.shape[1])


def on_device(glu_input, depth_kernel, norm_scale, norm_shift, proj_weight, out_grad):
    width = proj_weight.shape[1]
    rows = proj_weight.shape[0]
    frames = glu_input.shape[1]
    taps = depth_kernel.shape[0]
    radius = (taps - 1) // 2
    peers = lax.axis_size("tensor")
    me = lax.axis_index("tensor")
    local = glu_input.shape[0] * frames
    everyone = local * lax.axis_size("dp") * peers
    flat_grad = out_grad.reshape(-1, width)
    group_grad = lax.all_gather(flat_grad, "tensor", axis=0, tiled=True)
    values = glu_input[..., :width].astype(jnp.float32)
    gates = jax.nn.sigmoid(glu_input[..., width:].astype(jnp.float32))
    gated = (values * gates).astype(jnp.bfloat16)
    padded = extended(gated, (("tensor", 1),), radius)
    conv_out = jnp.zeros(gated.shape, jnp.float32)
    for offset in range(taps):
        conv_out = conv_out + depth_kernel[offset] * padded[:, offset : offset + frames, :]
    mean_local = jnp.sum(conv_out, axis=(0, 1)) / local
    dev_local = conv_out - mean_local
    spread_local = jnp.sum(dev_local * dev_local, axis=(0, 1))
    if all((is_power_of_two(lax.axis_size(a)) for a in ("dp", "tensor"))):
        average, spread = all_moments(mean_local, spread_local, float(local), ("dp", "tensor"))
        variance = spread / everyone
    else:
        average = lax.psum(jnp.sum(conv_out, axis=(0, 1)), ("dp", "tensor")) / everyone
        centred0 = conv_out - average
        variance = lax.psum(jnp.sum(centred0 * centred0, axis=(0, 1)), ("dp", "tensor")) / everyone
    group_grad, average = lax.optimization_barrier((group_grad, average))
    own_columns = jnp.einsum(
        "fd,cd->fc", group_grad, proj_weight, preferred_element_type=jnp.float32
    )
    grad_act = lax.all_to_all(own_columns, "tensor", split_axis=0, concat_axis=1, tiled=True)
    grad_act = grad_act.reshape(out_grad.shape)
    centred = conv_out - average
    inverse = lax.rsqrt(variance + epsilon)
    normed = centred * inverse
    affine = norm_scale * normed + norm_shift
    sig_affine = jax.nn.sigmoid(affine)
    activated = (affine * sig_affine).astype(jnp.bfloat16)
    flat_act = activated.reshape(-1, width)
    group_act = lax.all_to_all(flat_act, "tensor", split_axis=1, concat_axis=0, tiled=True)
    local_grad = jnp.einsum("fc,fd->cd", group_act, group_grad, preferred_element_type=jnp.float32)
    grad_affine = grad_act * (sig_affine + affine * sig_affine * (1.0 - sig_affine))
    sums = jnp.stack(
        [jnp.sum(grad_affine, axis=(0, 1)), jnp.sum(grad_affine * normed, axis=(0, 1))]
    )
    sums = all_sum(sums, ("tensor", "dp"))
    shift_grad, scale_grad = (sums[0], sums[1])
    grad_conv = (
        norm_scale
        * inverse
        * (grad_affine - shift_grad / everyone - normed * scale_grad / everyone)
    ).astype(jnp.bfloat16)
    grad_pad = extended(grad_conv, (("tensor", 1),), radius)
    grad_gated = jnp.zeros(gated.shape, jnp.float32)
    for offset in range(taps):
        begin = 2 * radius - offset
        grad_gated = grad_gated + depth_kernel[offset] * grad_pad[:, begin : begin + frames, :]
    grad_wide = grad_conv.astype(jnp.float32)
    kernel_terms = jnp.stack(
        [
            jnp.sum(
                padded[:, offset : offset + frames, :].astype(jnp.float32) * grad_wide, axis=(0, 1)
            )
            for offset in range(taps)
        ]
    )
    weight_grad = rows_sum(local_grad, "dp")
    kernel_grad = all_sum(kernel_terms, ("dp", "tensor"))
    input_grad = jnp.concatenate(
        [grad_gated * gates, grad_gated * values * gates * (1.0 - gates)], axis=-1
    ).astype(jnp.bfloat16)
    full_weight = gather_weight(proj_weight)
    conv_output = jnp.einsum(
        "btc,cd->btd", activated, full_weight, preferred_element_type=jnp.float32
    ).astype(jnp.bfloat16)
    return (conv_output, input_grad, weight_grad, kernel_grad, scale_grad, shift_grad)


def solution(mesh):
    in_specs = (P("dp", "tensor", None), P(), P(), P(), P("tensor", None), P("dp", "tensor", None))
    out_specs = (P("dp", "tensor", None), P("dp", "tensor", None), P("tensor", None), P(), P(), P())
    return jax.shard_map(
        on_device, mesh=mesh, in_specs=in_specs, out_specs=out_specs, check_vma=False
    )
```

profile of v0, /device:TPU:0, one launch (start us, length us, event | category | flops | bytes accessed | tf_op | source)
XLA Modules:
  0.0 186.6 jit_solution(8996814178643198088)
XLA Ops:
  7.9 1.3 fusion
  9.3 4.9 %collective-permute-start = (bf16[2,15,1536]{2,1,0:T(8,128)(2,1)S(1)}, bf16[2,15,1536]{2,1,0:T(8,128)(2,1)S(1)}, u32[]{:S(2)}, u32[]{:S(2)}) collective-permute-start(bf16[2,15,1536]{2,1,0:T(8,128)(2,1)S(1)} %get-tuple-element.99), channel_id=1, source_target_pairs={{0,1},{1,2},{2,3},{4,5},{5,6},{6,7},{8,9},{9,10},{10,11},{12,13},{... | collective-permute-start | bytes 276488 | tf_op jit(solution)/shard_map/ppermute | solution.py:16
  14.2 1.3 collective-permute-start.1
  16.4 4.3 %collective-permute-done.1 = bf16[2,15,1536]{2,1,0:T(8,128)(2,1)S(1)} collective-permute-done((bf16[2,15,1536]{2,1,0:T(8,128)(2,1)S(1)}, bf16[2,15,1536]{2,1,0:T(8,128)(2,1)S(1)}, u32[]{:S(2)}, u32[]{:S(2)}) %collective-permute-start.1) | collective-permute-done | bytes 92192 | tf_op jit(solution)/shard_map/ppermute | solution.py:17
  20.7 3.8 %fusion.143 = (f32[1536]{0:T(1024)S(1)}, f32[2,64,1536]{2,1,0:T(8,128)S(1)}) fusion(bf16[2,15,1536]{2,1,0:T(8,128)(2,1)S(1)} %collective-permute-done.1, bf16[2,64,1536]{2,1,0:T(8,128)(2,1)S(1)} %fusion, f32[1536]{0:T(1024)S(1)} %get-tuple-element.72, f32[1536]{0:T(1024)S(1)} %get-tuple-element.73, f32[1536]{0:T(1024)S(1)} %get-tuple-element.44, ...), kind=kLoop, calls=%fused_computation.380 | loop fusion | flops 35977728 | bytes 1560576 | tf_op jit(solution)/shard_map/reduce_sum | solution.py:109
  24.9 1.2 collective-permute-done.2
  26.1 1.6 collective-permute-start.3
  27.7 2.2 %collective-permute-done.3 = f32[2,1536]{1,0:T(2,128)S(1)} collective-permute-done((f32[2,1536]{1,0:T(2,128)S(1)}, f32[2,1536]{1,0:T(2,128)S(1)}, u32[]{:S(2)}, u32[]{:S(2)}) %collective-permute-start.3) | collective-permute-done | bytes 12320 | tf_op jit(solution)/shard_map/ppermute | solution.py:44
  29.9 1.6 collective-permute-start.4
  31.5 2.2 %collective-permute-done.4 = f32[2,1536]{1,0:T(2,128)S(1)} collective-permute-done((f32[2,1536]{1,0:T(2,128)S(1)}, f32[2,1536]{1,0:T(2,128)S(1)}, u32[]{:S(2)}, u32[]{:S(2)}) %collective-permute-start.4) | collective-permute-done | bytes 12320 | tf_op jit(solution)/shard_map/ppermute | solution.py:44
  33.8 1.6 collective-permute-start.5
  35.4 2.5 %collective-permute-done.5 = f32[2,1536]{1,0:T(2,128)S(1)} collective-permute-done((f32[2,1536]{1,0:T(2,128)S(1)}, f32[2,1536]{1,0:T(2,128)S(1)}, u32[]{:S(2)}, u32[]{:S(2)}) %collective-permute-start.5) | collective-permute-done | bytes 12320 | tf_op jit(solution)/shard_map/ppermute | solution.py:44
  38.0 2.5 %collective-permute-start.6 = (f32[2,1536]{1,0:T(2,128)S(1)}, f32[2,1536]{1,0:T(2,128)S(1)}, u32[]{:S(2)}, u32[]{:S(2)}) collective-permute-start(f32[2,1536]{1,0:T(2,128)S(1)} %pad_maximum_fusion.10), channel_id=1, source_target_pairs={{0,2},{1,3},{2,0},{3,1},{4,6},{5,7},{6,4},{7,5},{8,10},{9,11},{10,... | collective-permute-start | bytes 36872 | tf_op jit(solution)/shard_map/ppermute | solution.py:44
  40.5 2.9 %collective-permute-done.6 = f32[2,1536]{1,0:T(2,128)S(1)} collective-permute-done((f32[2,1536]{1,0:T(2,128)S(1)}, f32[2,1536]{1,0:T(2,128)S(1)}, u32[]{:S(2)}, u32[]{:S(2)}) %collective-permute-start.6) | collective-permute-done | bytes 12320 | tf_op jit(solution)/shard_map/ppermute | solution.py:44
  44.2 5.8 %all-gather.4.cloned.1.call-done = bf16[512,1536]{1,0:T(8,128)(2,1)} async-done(((bf16[128,1536]{1,0:T(8,128)(2,1)}), bf16[512,1536]{1,0:T(8,128)(2,1)}) %all-gather.4.cloned.1.call-update) | async-done | bytes 1572880 | tf_op jit(solution)/shard_map/all_gather | solution.py:101
  50.0 2.4 %fusion.147 = f32[512,384]{1,0:T(8,128)S(1)} fusion(bf16[512,1536]{1,0:T(8,128)(2,1)} %all-gather.4.cloned.1.call-done, bf16[384,1536]{1,0:T(8,128)(2,1)S(1)} %copy-done), kind=kOutput, calls=%fused_computation.383 | convolution fusion | flops 603979776 | bytes 3538944 | tf_op jit(solution)/shard_map/fd,cd->fc/dot_general | solution.py:120
  52.4 22.6 %all_to_all.35 = f32[4,128,384]{2,1,0:T(8,128)S(1)} all-to-all(f32[4,128,384]{2,1,0:T(8,128)S(1)} %bitcast.21), channel_id=1, replica_groups=mesh['dp'=8,'tensor'=4] {'tensor'}, dimensions={0} | all-to-all | bytes 1572864 | tf_op jit(solution)/shard_map/all_to_all | solution.py:123
  75.6 1.2 reshape.189
  76.8 2.4 %fusion.140 = (f32[1536]{0:T(1024)S(1)}, f32[1536]{0:T(1024)S(1)}, f32[2,64,1536]{2,1,0:T(8,128)}, bf16[2,64,1536]{2,1,0:T(8,128)(2,1)S(1)}) fusion(f32[1536]{0:T(1024)S(1)} %get-tuple-element.90, f32[2,64,1536]{2,1,0:T(8,128)S(1)} %get-tuple-element.93, f32[1536]{0:T(1024)S(1)} %get-tuple-element.8, f32[2,64,1536]{2,1,0:T(8,128)} %reshape.189, ...), kind=kLoop, calls=%fused_computation.378 | loop fusion | flops 3142656 | bytes 2789376 | tf_op jit(solution)/shard_map/reduce_sum | solution.py:136
  80.4 3.5 %all-to-all-start.1 = ((bf16[128,4,384]{2,0,1:T(8,128)(2,1)}), bf16[128,4,384]{2,0,1:T(8,128)(2,1)S(1)}, u32[]{:S(2)}, u32[]{:S(2)}) async-start(bf16[128,4,384]{2,0,1:T(8,128)(2,1)} %copy.17), calls=%async_computation.1 | async-start | bytes 786432 | tf_op jit(solution)/shard_map/all_to_all | solution.py:132
  84.2 2.7 %collective-permute-start.9 = (f32[2,1536]{1,0:T(2,128)S(1)}, f32[2,1536]{1,0:T(2,128)S(1)}, u32[]{:S(2)}, u32[]{:S(2)}) collective-permute-start(f32[2,1536]{1,0:T(2,128)S(1)} %fusion.139), channel_id=1, source_target_pairs={{0,2},{1,3},{2,0},{3,1},{4,6},{5,7},{6,4},{7,5},{8,10},{9,11},{10,... | collective-permute-start | bytes 36872 | tf_op jit(solution)/shard_map/ppermute | solution.py:34
  87.8 7.6 %collective-permute-done.9 = f32[2,1536]{1,0:T(2,128)S(1)} collective-permute-done((f32[2,1536]{1,0:T(2,128)S(1)}, f32[2,1536]{1,0:T(2,128)S(1)}, u32[]{:S(2)}, u32[]{:S(2)}) %collective-permute-start.9) | collective-permute-done | bytes 12320 | tf_op jit(solution)/shard_map/ppermute | solution.py:34
  95.5 1.2 collective-permute-done.10
  96.7 1.5 collective-permute-start.11
  98.2 2.2 %collective-permute-done.11 = f32[2,1536]{1,0:T(2,128)S(1)} collective-permute-done((f32[2,1536]{1,0:T(2,128)S(1)}, f32[2,1536]{1,0:T(2,128)S(1)}, u32[]{:S(2)}, u32[]{:S(2)}) %collective-permute-start.11) | collective-permute-done | bytes 12320 | tf_op jit(solution)/shard_map/ppermute | solution.py:34
  100.5 1.5 collective-permute-start.12
  102.0 2.2 %collective-permute-done.12 = f32[2,1536]{1,0:T(2,128)S(1)} collective-permute-done((f32[2,1536]{1,0:T(2,128)S(1)}, f32[2,1536]{1,0:T(2,128)S(1)}, u32[]{:S(2)}, u32[]{:S(2)}) %collective-permute-start.12) | collective-permute-done | bytes 12320 | tf_op jit(solution)/shard_map/ppermute | solution.py:34
  104.2 2.2 %fusion.148 = f32[384,1536]{1,0:T(8,128)S(1)} fusion(bf16[512,384]{1,0:T(8,128)(2,1)S(1)} %bitcast.20, bf16[512,1536]{1,0:T(8,128)(2,1)} %all-gather.4.cloned.1.call-done), kind=kOutput, calls=%fused_computation.384 | convolution fusion | flops 603979776 | bytes 4325376 | tf_op jit(solution)/shard_map/fc,fd->cd/dot_general | solution.py:133
  107.6 1.5 fusion.80
  109.2 1.2 fusion.64
  110.5 1.0 copy-done.2
  112.4 1.5 collective-permute-start.16
  121.1 2.5 %stack.172 = f32[31,1536]{1,0:T(8,128)S(1)} concatenate(f32[1,1536]{1,0:T(1,128)} %stack.141, f32[1,1536]{1,0:T(1,128)} %stack.142, f32[1,1536]{1,0:T(1,128)} %stack.143, f32[1,1536]{1,0:T(1,128)} %stack.144, f32[1,1536]{1,0:T(1,128)} %stack.145, f32[1,1536]{1,0:T(1,128)S(1)} %stack.146, f32[1,1536]{1,0:T(1,128)S(1)} %stack.147, f32[1,1536]{1,0:T(1,128)S(1)} %stack.148, ...), dimensions={0} | concatenate | bytes 380928 | tf_op jit(solution)/shard_map/stack | solution.py:151
  123.8 14.4 %all-gather.6.cloned.1.call-done = bf16[768,1536]{1,0:T(8,128)(2,1)} async-done(((bf16[192,1536]{1,0:T(8,128)(2,1)}), bf16[768,1536]{1,0:T(8,128)(2,1)}) %all-gather.6.cloned.1.call-update) | async-done | bytes 2359312 | tf_op jit(solution)/shard_map/all_gather | solution.py:83
  138.2 1.5 collective-permute-start.22
  139.8 1.1 dynamic-slice_add_fusion.1
  141.2 1.5 collective-permute-start.17
  142.8 1.3 collective-permute-start.13
  144.1 4.6 %collective-permute-start.14 = (bf16[2,15,1536]{2,1,0:T(8,128)(2,1)S(1)}, bf16[2,15,1536]{2,1,0:T(8,128)(2,1)S(1)}, u32[]{:S(2)}, u32[]{:S(2)}) collective-permute-start(bf16[2,15,1536]{2,1,0:T(8,128)(2,1)S(1)} %get-tuple-element.98), channel_id=1, source_target_pairs={{0,1},{1,2},{2,3},{4,5},{5,6},{6,7},{8,9},{9,10},{10,11},{12,13},{... | collective-permute-start | bytes 276488 | tf_op jit(solution)/shard_map/ppermute | solution.py:16
  149.3 1.1 collective-permute-done.17
  150.5 2.1 %collective-permute-start.18 = (f32[48,1536]{1,0:T(8,128)S(1)}, f32[48,1536]{1,0:T(8,128)S(1)}, u32[]{:S(2)}, u32[]{:S(2)}) collective-permute-start(f32[48,1536]{1,0:T(8,128)S(1)} %dynamic-slice_add_fusion.2), channel_id=1, source_target_pairs={{0,16},{4,20},{8,24},{12,28},{16,0},{20,4},{24,8},{28,12},{1,17},{... | collective-permute-start | bytes 884744 | tf_op jit(solution)/shard_map/ppermute | solution.py:71
  152.9 4.1 %multiply_convert_fusion = (bf16[2,64,1536]{2,1,0:T(8,128)(2,1)S(1)}, f32[2,64,1536]{2,1,0:T(8,128)S(1)}) fusion(bf16[2,64,3072]{2,1,0:T(8,128)(2,1)S(1)} %copy-done.1, bf16[2,64,1536]{2,1,0:T(8,128)(2,1)S(1)} %get-tuple-element.86, bf16[2,15,1536]{2,1,0:T(8,128)(2,1)S(1)} %collective-permute-done.14, f32[1536]{0:T(1024)S(1)} %copy-done.62, ...), kind=kLoop, calls=%fused_computation.210 | loop fusion | flops 36962304 | bytes 2340864 | tf_op jit(solution)/shard_map/convert
  157.7 3.6 %collective-permute-done.18 = f32[48,1536]{1,0:T(8,128)S(1)} collective-permute-done((f32[48,1536]{1,0:T(8,128)S(1)}, f32[48,1536]{1,0:T(8,128)S(1)}, u32[]{:S(2)}, u32[]{:S(2)}) %collective-permute-start.18) | collective-permute-done | bytes 294944 | tf_op jit(solution)/shard_map/ppermute | solution.py:71
  162.7 1.3 collective-permute-start.25
  165.0 7.5 %collective-permute-done.25 = f32[31,1536]{1,0:T(8,128)S(1)} collective-permute-done((f32[31,1536]{1,0:T(8,128)S(1)}, f32[31,1536]{1,0:T(8,128)S(1)}, u32[]{:S(2)}, u32[]{:S(2)}) %collective-permute-start.25) | collective-permute-done | bytes 190496 | tf_op jit(solution)/shard_map/ppermute | solution.py:34
  173.2 1.9 %collective-permute-done.19 = f32[96,1536]{1,0:T(8,128)S(1)} collective-permute-done((f32[96,1536]{1,0:T(8,128)S(1)}, f32[96,1536]{1,0:T(8,128)S(1)}, u32[]{:S(2)}, u32[]{:S(2)}) %collective-permute-start.19) | collective-permute-done | bytes 589856 | tf_op jit(solution)/shard_map/ppermute | solution.py:71
  175.9 1.5 convolution_convert_fusion
  178.1 1.6 maximum_select_fusion
  (250 shorter events, 21.0 us)
Async XLA Ops:
  7.2 42.8 %copy-start = (bf16[384,1536]{1,0:T(8,128)(2,1)S(1)}, bf16[384,1536]{1,0:T(8,128)(2,1)}, u32[]{:S(2)}) copy-start(bf16[384,1536]{1,0:T(8,128)(2,1)} %param.10) | copy-start | bytes 3538948
  7.2 42.8 %all-gather.4.cloned.1.call-start = ((), (), s32[]{:S(2)}) async-start(), calls=%async_computation.2 | async-start | bytes 1966080 | tf_op jit(solution)/shard_map/all_gather | solution.py:101
  9.3 7.1 %collective-permute-start = (bf16[2,15,1536]{2,1,0:T(8,128)(2,1)S(1)}, bf16[2,15,1536]{2,1,0:T(8,128)(2,1)S(1)}, u32[]{:S(2)}, u32[]{:S(2)}) collective-permute-start(bf16[2,15,1536]{2,1,0:T(8,128)(2,1)S(1)} %get-tuple-element.99), channel_id=1, source_target_pairs={{0,1},{1,2},{2,3},{4,5},{5,6},{6,7},{8,9},{9,10},{10,11},{12,13},{... | collective-permute-start | bytes 276488 | tf_op jit(solution)/shard_map/ppermute | solution.py:16
  14.2 6.5 %collective-permute-start.1 = (bf16[2,15,1536]{2,1,0:T(8,128)(2,1)S(1)}, bf16[2,15,1536]{2,1,0:T(8,128)(2,1)S(1)}, u32[]{:S(2)}, u32[]{:S(2)}) collective-permute-start(bf16[2,15,1536]{2,1,0:T(8,128)(2,1)S(1)} %get-tuple-element.100), channel_id=1, source_target_pairs={{1,0},{2,1},{3,2},{5,4},{6,5},{7,6},{9,8},{10,9},{11,10},{13,12},{... | collective-permute-start | bytes 276488 | tf_op jit(solution)/shard_map/ppermute | solution.py:17
  15.9 28.2 %copy-start.7 = (f32[1536]{0:T(1024)}, f32[1536]{0:T(1024)S(1)}, u32[]{:S(2)}) copy-start(f32[1536]{0:T(1024)S(1)} %get-tuple-element.45) | copy-start | bytes 18436
  15.9 28.2 %copy-start.9 = (f32[1536]{0:T(1024)}, f32[1536]{0:T(1024)S(1)}, u32[]{:S(2)}) copy-start(f32[1536]{0:T(1024)S(1)} %get-tuple-element.46) | copy-start | bytes 18436
  15.9 28.2 %copy-start.11 = (f32[1536]{0:T(1024)}, f32[1536]{0:T(1024)S(1)}, u32[]{:S(2)}) copy-start(f32[1536]{0:T(1024)S(1)} %get-tuple-element.47) | copy-start | bytes 18436
  15.9 28.2 %copy-start.13 = (f32[1536]{0:T(1024)}, f32[1536]{0:T(1024)S(1)}, u32[]{:S(2)}) copy-start(f32[1536]{0:T(1024)S(1)} %get-tuple-element.48) | copy-start | bytes 18436
  15.9 28.1 %copy-start.15 = (f32[1536]{0:T(1024)}, f32[1536]{0:T(1024)S(1)}, u32[]{:S(2)}) copy-start(f32[1536]{0:T(1024)S(1)} %get-tuple-element.49) | copy-start | bytes 18436
  15.9 28.1 %copy-start.17 = (f32[1536]{0:T(1024)}, f32[1536]{0:T(1024)S(1)}, u32[]{:S(2)}) copy-start(f32[1536]{0:T(1024)S(1)} %get-tuple-element.50) | copy-start | bytes 18436
  15.9 28.1 %copy-start.19 = (f32[1536]{0:T(1024)}, f32[1536]{0:T(1024)S(1)}, u32[]{:S(2)}) copy-start(f32[1536]{0:T(1024)S(1)} %get-tuple-element.51) | copy-start | bytes 18436
  15.9 28.1 %copy-start.21 = (f32[1536]{0:T(1024)}, f32[1536]{0:T(1024)S(1)}, u32[]{:S(2)}) copy-start(f32[1536]{0:T(1024)S(1)} %get-tuple-element.52) | copy-start | bytes 18436
  15.9 28.1 %copy-start.23 = (f32[1536]{0:T(1024)}, f32[1536]{0:T(1024)S(1)}, u32[]{:S(2)}) copy-start(f32[1536]{0:T(1024)S(1)} %get-tuple-element.53) | copy-start | bytes 18436
  16.0 28.1 %copy-start.25 = (f32[1536]{0:T(1024)}, f32[1536]{0:T(1024)S(1)}, u32[]{:S(2)}) copy-start(f32[1536]{0:T(1024)S(1)} %get-tuple-element.54) | copy-start | bytes 18436
  16.3 33.7 %copy-start.59 = (f32[1536]{0:T(1024)}, f32[1536]{0:T(1024)S(1)}, u32[]{:S(2)}) copy-start(f32[1536]{0:T(1024)S(1)} %get-tuple-element.71) | copy-start | bytes 18436
  16.3 33.7 %copy-start.61 = (f32[1536]{0:T(1024)}, f32[1536]{0:T(1024)S(1)}, u32[]{:S(2)}) copy-start(f32[1536]{0:T(1024)S(1)} %get-tuple-element.72) | copy-start | bytes 18436
  16.3 33.6 %copy-start.63 = (f32[1536]{0:T(1024)}, f32[1536]{0:T(1024)S(1)}, u32[]{:S(2)}) copy-start(f32[1536]{0:T(1024)S(1)} %get-tuple-element.73) | copy-start | bytes 18436
  16.3 36.0 %copy-start.45 = (f32[1536]{0:T(1024)}, f32[1536]{0:T(1024)S(1)}, u32[]{:S(2)}) copy-start(f32[1536]{0:T(1024)S(1)} %get-tuple-element.64) | copy-start | bytes 18436
  16.3 36.0 %copy-start.47 = (f32[1536]{0:T(1024)}, f32[1536]{0:T(1024)S(1)}, u32[]{:S(2)}) copy-start(f32[1536]{0:T(1024)S(1)} %get-tuple-element.65) | copy-start | bytes 18436
  16.3 36.0 %copy-start.49 = (f32[1536]{0:T(1024)}, f32[1536]{0:T(1024)S(1)}, u32[]{:S(2)}) copy-start(f32[1536]{0:T(1024)S(1)} %get-tuple-element.66) | copy-start | bytes 18436
  16.3 36.0 %copy-start.51 = (f32[1536]{0:T(1024)}, f32[1536]{0:T(1024)S(1)}, u32[]{:S(2)}) copy-start(f32[1536]{0:T(1024)S(1)} %get-tuple-element.67) | copy-start | bytes 18436
  16.4 36.0 %copy-start.53 = (f32[1536]{0:T(1024)}, f32[1536]{0:T(1024)S(1)}, u32[]{:S(2)}) copy-start(f32[1536]{0:T(1024)S(1)} %get-tuple-element.68) | copy-start | bytes 18436
  24.8 1.2 collective-permute-start.2
  26.1 3.8 %collective-permute-start.3 = (f32[2,1536]{1,0:T(2,128)S(1)}, f32[2,1536]{1,0:T(2,128)S(1)}, u32[]{:S(2)}, u32[]{:S(2)}) collective-permute-start(f32[2,1536]{1,0:T(2,128)S(1)} %pad_maximum_fusion.7), channel_id=1, source_target_pairs={{0,8},{4,12},{8,0},{12,4},{16,24},{20,28},{24,16},{28,20},{1,9},{5... | collective-permute-start | bytes 36872 | tf_op jit(solution)/shard_map/ppermute | solution.py:44
  29.9 3.8 %collective-permute-start.4 = (f32[2,1536]{1,0:T(2,128)S(1)}, f32[2,1536]{1,0:T(2,128)S(1)}, u32[]{:S(2)}, u32[]{:S(2)}) collective-permute-start(f32[2,1536]{1,0:T(2,128)S(1)} %pad_maximum_fusion.8), channel_id=1, source_target_pairs={{0,16},{4,20},{8,24},{12,28},{16,0},{20,4},{24,8},{28,12},{1,17},{... | collective-permute-start | bytes 36872 | tf_op jit(solution)/shard_map/ppermute | solution.py:44
  33.8 4.2 %collective-permute-start.5 = (f32[2,1536]{1,0:T(2,128)S(1)}, f32[2,1536]{1,0:T(2,128)S(1)}, u32[]{:S(2)}, u32[]{:S(2)}) collective-permute-start(f32[2,1536]{1,0:T(2,128)S(1)} %pad_maximum_fusion.9), channel_id=1, source_target_pairs={{0,1},{1,0},{2,3},{3,2},{4,5},{5,4},{6,7},{7,6},{8,9},{9,8},{10,11... | collective-permute-start | bytes 36872 | tf_op jit(solution)/shard_map/ppermute | solution.py:44
  38.0 5.4 %collective-permute-start.6 = (f32[2,1536]{1,0:T(2,128)S(1)}, f32[2,1536]{1,0:T(2,128)S(1)}, u32[]{:S(2)}, u32[]{:S(2)}) collective-permute-start(f32[2,1536]{1,0:T(2,128)S(1)} %pad_maximum_fusion.10), channel_id=1, source_target_pairs={{0,2},{1,3},{2,0},{3,1},{4,6},{5,7},{6,4},{7,5},{8,10},{9,11},{10,... | collective-permute-start | bytes 36872 | tf_op jit(solution)/shard_map/ppermute | solution.py:44
  79.3 4.9 %collective-permute-start.8 = (f32[2,1536]{1,0:T(2,128)S(1)}, f32[2,1536]{1,0:T(2,128)S(1)}, u32[]{:S(2)}, u32[]{:S(2)}) collective-permute-start(f32[2,1536]{1,0:T(2,128)S(1)} %pad_maximum_fusion.11), channel_id=1, source_target_pairs={{0,1},{1,0},{2,3},{3,2},{4,5},{5,4},{6,7},{7,6},{8,9},{9,8},{10,11... | collective-permute-start | bytes 36872 | tf_op jit(solution)/shard_map/ppermute | solution.py:34
  80.4 23.8 %all-to-all-start.1 = ((bf16[128,4,384]{2,0,1:T(8,128)(2,1)}), bf16[128,4,384]{2,0,1:T(8,128)(2,1)S(1)}, u32[]{:S(2)}, u32[]{:S(2)}) async-start(bf16[128,4,384]{2,0,1:T(8,128)(2,1)} %copy.17), calls=%async_computation.1 | async-start | bytes 786432 | tf_op jit(solution)/shard_map/all_to_all | solution.py:132
  83.9 54.3 %all-gather.6.cloned.1.call-start = ((), (), s32[]{:S(2)}) async-start(), calls=%async_computation.3 | async-start | bytes 2949120 | tf_op jit(solution)/shard_map/all_gather | solution.py:83
  84.2 11.2 %collective-permute-start.9 = (f32[2,1536]{1,0:T(2,128)S(1)}, f32[2,1536]{1,0:T(2,128)S(1)}, u32[]{:S(2)}, u32[]{:S(2)}) collective-permute-start(f32[2,1536]{1,0:T(2,128)S(1)} %fusion.139), channel_id=1, source_target_pairs={{0,2},{1,3},{2,0},{3,1},{4,6},{5,7},{6,4},{7,5},{8,10},{9,11},{10,... | collective-permute-start | bytes 36872 | tf_op jit(solution)/shard_map/ppermute | solution.py:34
  95.4 1.2 collective-permute-start.10
  96.7 3.8 %collective-permute-start.11 = (f32[2,1536]{1,0:T(2,128)S(1)}, f32[2,1536]{1,0:T(2,128)S(1)}, u32[]{:S(2)}, u32[]{:S(2)}) collective-permute-start(f32[2,1536]{1,0:T(2,128)S(1)} %add.496), channel_id=1, source_target_pairs={{0,8},{4,12},{8,0},{12,4},{16,24},{20,28},{24,16},{28,20},{1,9},{5... | collective-permute-start | bytes 36872 | tf_op jit(solution)/shard_map/ppermute | solution.py:34
  100.5 3.8 %collective-permute-start.12 = (f32[2,1536]{1,0:T(2,128)S(1)}, f32[2,1536]{1,0:T(2,128)S(1)}, u32[]{:S(2)}, u32[]{:S(2)}) collective-permute-start(f32[2,1536]{1,0:T(2,128)S(1)} %add.497), channel_id=1, source_target_pairs={{0,16},{4,20},{8,24},{12,28},{16,0},{20,4},{24,8},{28,12},{1,17},{... | collective-permute-start | bytes 36872 | tf_op jit(solution)/shard_map/ppermute | solution.py:34
  106.6 3.8 %collective-permute-start.15 = (f32[192,1536]{1,0:T(8,128)S(1)}, f32[192,1536]{1,0:T(8,128)S(1)}, u32[]{:S(2)}, u32[]{:S(2)}) collective-permute-start(f32[192,1536]{1,0:T(8,128)S(1)} %constant_dynamic-slice_fusion.2), channel_id=1, source_target_pairs={{0,4},{4,0},{8,12},{12,8},{16,20},{20,16},{24,28},{28,24},{1,5},{5... | collective-permute-start | bytes 3538952 | tf_op jit(solution)/shard_map/ppermute | solution.py:67
  112.4 27.4 %collective-permute-start.16 = (f32[96,1536]{1,0:T(8,128)}, f32[96,1536]{1,0:T(8,128)}, u32[]{:S(2)}, u32[]{:S(2)}) collective-permute-start(f32[96,1536]{1,0:T(8,128)} %constant_dynamic-slice_fusion.1), channel_id=1, source_target_pairs={{0,8},{4,12},{8,0},{12,4},{16,24},{20,28},{24,16},{28,20},{1,9},{5... | collective-permute-start | bytes 1769480 | tf_op jit(solution)/shard_map/ppermute | solution.py:67
  123.6 14.6 %collective-permute-start.21 = (f32[31,1536]{1,0:T(8,128)S(1)}, f32[31,1536]{1,0:T(8,128)S(1)}, u32[]{:S(2)}, u32[]{:S(2)}) collective-permute-start(f32[31,1536]{1,0:T(8,128)S(1)} %stack.172), channel_id=1, source_target_pairs={{0,4},{4,0},{8,12},{12,8},{16,20},{20,16},{24,28},{28,24},{1,5},{5... | collective-permute-start | bytes 571400 | tf_op jit(solution)/shard_map/ppermute | solution.py:34
  138.2 37.1 %collective-permute-start.7 = (bf16[4,192,1536]{2,1,0:T(8,128)(2,1)}, bf16[4,192,1536]{2,1,0:T(8,128)(2,1)S(1)}, u32[]{:S(2)}, u32[]{:S(2)}) collective-permute-start(bf16[4,192,1536]{2,1,0:T(8,128)(2,1)} %bitcast.18), channel_id=1, source_target_pairs={{0,4},{4,0},{8,12},{12,8},{16,20},{20,16},{24,28},{28,24},{1,5},{5... | collective-permute-start | bytes 7077896 | tf_op jit(solution)/shard_map/ppermute | solution.py:84
  138.2 10.4 %collective-permute-start.22 = (f32[31,1536]{1,0:T(8,128)S(1)}, f32[31,1536]{1,0:T(8,128)S(1)}, u32[]{:S(2)}, u32[]{:S(2)}) collective-permute-start(f32[31,1536]{1,0:T(8,128)S(1)} %add.537), channel_id=1, source_target_pairs={{0,8},{4,12},{8,0},{12,4},{16,24},{20,28},{24,16},{28,20},{1,9},{5... | collective-permute-start | bytes 571400 | tf_op jit(solution)/shard_map/ppermute | solution.py:34
  141.2 9.2 %collective-permute-start.17 = (f32[48,1536]{1,0:T(8,128)S(1)}, f32[48,1536]{1,0:T(8,128)S(1)}, u32[]{:S(2)}, u32[]{:S(2)}) collective-permute-start(f32[48,1536]{1,0:T(8,128)S(1)} %constant_dynamic-slice_fusion), channel_id=1, source_target_pairs={{0,16},{4,20},{8,24},{12,28},{16,0},{20,4},{24,8},{28,12},{1,17},{... | collective-permute-start | bytes 884744 | tf_op jit(solution)/shard_map/ppermute | solution.py:67
  142.8 9.8 %collective-permute-start.13 = (bf16[2,15,1536]{2,1,0:T(8,128)(2,1)S(1)}, bf16[2,15,1536]{2,1,0:T(8,128)(2,1)S(1)}, u32[]{:S(2)}, u32[]{:S(2)}) collective-permute-start(bf16[2,15,1536]{2,1,0:T(8,128)(2,1)S(1)} %get-tuple-element.97), channel_id=1, source_target_pairs={{1,0},{2,1},{3,2},{5,4},{6,5},{7,6},{9,8},{10,9},{11,10},{13,12},{... | collective-permute-start | bytes 276488 | tf_op jit(solution)/shard_map/ppermute | solution.py:17
  144.1 8.5 %collective-permute-start.14 = (bf16[2,15,1536]{2,1,0:T(8,128)(2,1)S(1)}, bf16[2,15,1536]{2,1,0:T(8,128)(2,1)S(1)}, u32[]{:S(2)}, u32[]{:S(2)}) collective-permute-start(bf16[2,15,1536]{2,1,0:T(8,128)(2,1)S(1)} %get-tuple-element.98), channel_id=1, source_target_pairs={{0,1},{1,2},{2,3},{4,5},{5,6},{6,7},{8,9},{9,10},{10,11},{12,13},{... | collective-permute-start | bytes 276488 | tf_op jit(solution)/shard_map/ppermute | solution.py:16
  148.7 8.2 %collective-permute-start.23 = (f32[31,1536]{1,0:T(8,128)S(1)}, f32[31,1536]{1,0:T(8,128)S(1)}, u32[]{:S(2)}, u32[]{:S(2)}) collective-permute-start(f32[31,1536]{1,0:T(8,128)S(1)} %add.538), channel_id=1, source_target_pairs={{0,16},{4,20},{8,24},{12,28},{16,0},{20,4},{24,8},{28,12},{1,17},{... | collective-permute-start | bytes 571400 | tf_op jit(solution)/shard_map/ppermute | solution.py:34
  150.5 10.8 %collective-permute-start.18 = (f32[48,1536]{1,0:T(8,128)S(1)}, f32[48,1536]{1,0:T(8,128)S(1)}, u32[]{:S(2)}, u32[]{:S(2)}) collective-permute-start(f32[48,1536]{1,0:T(8,128)S(1)} %dynamic-slice_add_fusion.2), channel_id=1, source_target_pairs={{0,16},{4,20},{8,24},{12,28},{16,0},{20,4},{24,8},{28,12},{1,17},{... | collective-permute-start | bytes 884744 | tf_op jit(solution)/shard_map/ppermute | solution.py:71
  157.0 5.7 %collective-permute-start.24 = (f32[31,1536]{1,0:T(8,128)S(1)}, f32[31,1536]{1,0:T(8,128)S(1)}, u32[]{:S(2)}, u32[]{:S(2)}) collective-permute-start(f32[31,1536]{1,0:T(8,128)S(1)} %add.539), channel_id=1, source_target_pairs={{0,1},{1,0},{2,3},{3,2},{4,5},{5,4},{6,7},{7,6},{8,9},{9,8},{10,11... | collective-permute-start | bytes 571400 | tf_op jit(solution)/shard_map/ppermute | solution.py:34
  161.3 13.8 %collective-permute-start.19 = (f32[96,1536]{1,0:T(8,128)S(1)}, f32[96,1536]{1,0:T(8,128)S(1)}, u32[]{:S(2)}, u32[]{:S(2)}) collective-permute-start(f32[96,1536]{1,0:T(8,128)S(1)} %maximum_select_fusion.2), channel_id=1, source_target_pairs={{0,8},{4,12},{8,0},{12,4},{16,24},{20,28},{24,16},{28,20},{1,9},{5... | collective-permute-start | bytes 1769480 | tf_op jit(solution)/shard_map/ppermute | solution.py:71
  162.7 9.7 %collective-permute-start.25 = (f32[31,1536]{1,0:T(8,128)S(1)}, f32[31,1536]{1,0:T(8,128)S(1)}, u32[]{:S(2)}, u32[]{:S(2)}) collective-permute-start(f32[31,1536]{1,0:T(8,128)S(1)} %add.540), channel_id=1, source_target_pairs={{0,2},{1,3},{2,0},{3,1},{4,6},{5,7},{6,4},{7,5},{8,10},{9,11},{10,... | collective-permute-start | bytes 571400 | tf_op jit(solution)/shard_map/ppermute | solution.py:34
  175.2 2.9 %collective-permute-start.20 = (f32[192,1536]{1,0:T(8,128)S(1)}, f32[192,1536]{1,0:T(8,128)S(1)}, u32[]{:S(2)}, u32[]{:S(2)}) collective-permute-start(f32[192,1536]{1,0:T(8,128)S(1)} %maximum_select_fusion.1), channel_id=1, source_target_pairs={{0,4},{4,0},{8,12},{12,8},{16,20},{20,16},{24,28},{28,24},{1,5},{5... | collective-permute-start | bytes 3538952 | tf_op jit(solution)/shard_map/ppermute | solution.py:71
  (52 other events, 699.2 us)
Sparse Core Ops, SparseCore 0:
  9.6 40.3 all-gather.3
  87.9 50.2 all-gather.5
where the time goes:
time: 187 us
  waiting for transfers between devices  64.7 us (35%)
  starting transfers between devices  39.4 us (21%)
  other arithmetic  22.9 us (12%)
  blocking collectives  22.6 us (12%)
  between operations  15.7 us (8%)
  local copies, waits for them, and re-layouts  15.2 us (8%)
  matrix products  6.16 us (3%)
    all_to_all x1, blocking collectives, on_device(): lax.all_to_all(own_columns, 'tensor', split_axis=0, concat_axis=1, tiled=...  22.6 us
    ppermute x10, waiting for transfers between devices, all_sum(): x = x + lax.ppermute(x, axis, [(i, i ^ step) for i in range(peers)])  21.2 us
    all_gather x1, waiting for transfers between devices, gather_weight(): held = lax.all_gather(mine, 'tensor', axis=0, tiled=False)  14.4 us
    ppermute x5, waiting for transfers between devices, all_moments(): lax.ppermute(jnp.stack([mean, spread]), axis, [(i, i ^ step) for i in ran...  10.9 us
    ppermute x10, starting transfers between devices, all_sum(): x = x + lax.ppermute(x, axis, [(i, i ^ step) for i in range(peers)])  10.4 us
    ppermute x2, starting transfers between devices, extended(): before = lax.ppermute(last, axis, up)  9.48 us
    another operation x32, local copies, waits for them, and re-layouts, on_device(): jnp.stack([jnp.sum(padded[:, offset:offset + frames, :].astype(jnp.float3...  7.97 us
    ppermute x5, starting transfers between devices, all_moments(): lax.ppermute(jnp.stack([mean, spread]), axis, [(i, i ^ step) for i in ran...  7.35 us
  transfers between devices with their start and end apart: 29, of which 19 were waited for; matrix products, arithmetic and copies ran while one was open for 18% of the time, Pallas kernels for 0%

commit v1 on v0

--- a/solution.py
+++ b/solution.py
@@ -4,6 +4,12 @@
 from jax.sharding import PartitionSpec as P
 
 epsilon = 1e-05
+
+
+def laid_out(blocks, dim):
+    shape = list(blocks.shape[1:])
+    shape[dim] *= blocks.shape[0]
+    return jnp.moveaxis(blocks, 0, dim).reshape(shape)
 
 
 def extended(array, sides, width):
@@ -98,7 +104,19 @@
     local = glu_input.shape[0] * frames
     everyone = local * lax.axis_size("dp") * peers
     flat_grad = out_grad.reshape(-1, width)
-    group_grad = lax.all_gather(flat_grad, "tensor", axis=0, tiled=True)
+    size = lax.axis_size("tensor")
+    pairs = [(i_2, (i_2 + 1) % size) for i_2 in range(size)]
+    back = [(b, a_2) for a_2, b in pairs]
+    lower, upper = ([], [])
+    for k in range(size - 1):
+        if k % 2 == 0:
+            lower.append(lax.ppermute(lower[-1] if lower else flat_grad, "tensor", pairs))
+        else:
+            upper.append(lax.ppermute(upper[-1] if upper else flat_grad, "tensor", back))
+    parts = jnp.stack([*lower[::-1], flat_grad, *upper])
+    shift = lax.axis_index("tensor") - len(lower)
+    parts = parts[(jnp.arange(size) - shift) % size]
+    group_grad = laid_out(parts, 0)
     values = glu_input[..., :width].astype(jnp.float32)
     gates = jax.nn.sigmoid(glu_input[..., width:].astype(jnp.float32))
     gated = (values * gates).astype(jnp.bfloat16)

time: 187 us -> 209 us (1.12)
  waiting for transfers between devices: 64.7 us -> 82.6 us
  other arithmetic: 22.9 us -> 29.9 us
  local copies, waits for them, and re-layouts: 15.2 us -> 12.2 us
    ppermute x0 -> x3, waiting for transfers between devices: none -> 9.31 us  [the longest x2 9.31 us: on_device(): lax.ppermute(lower[-1] if lower else flat_grad, 'tensor', pairs)]
    ppermute x3, waiting for transfers between devices: 1.12 us -> 10.2 us  [rows_sum(): x = keep + lax.ppermute(give, axis, [(i, i ^ step) for i in range(peers)])]
    another operation x32, local copies, waits for them, and re-layouts: 7.97 us -> 0.52 us  [on_device(): jnp.stack([jnp.sum(padded[:, offset:offset + frames, :].astype(jnp.float3...]
    ppermute x5, waiting for transfers between devices: 10.9 us -> 17.5 us  [all_moments(): lax.ppermute(jnp.stack([mean, spread]), axis, [(i, i ^ step) for i in ran...]
    all_gather x1 -> x0, waiting for transfers between devices: 5.77 us -> none  [on_device(): group_grad = lax.all_gather(flat_grad, 'tensor', axis=0, tiled=True)]
    another operation x2 -> x3, other arithmetic: 4.36 us -> 10 us
    ppermute x3, waiting for transfers between devices: 6.13 us -> 1.06 us  [rows_sum(): other = lax.ppermute(x, axis, [(i, i ^ step) for i in range(peers)])]
    ppermute x10, starting transfers between devices: 10.4 us -> 6.5 us  [all_sum(): x = x + lax.ppermute(x, axis, [(i, i ^ step) for i in range(peers)])]
  transfers between devices with their start and end apart: 29 -> 31, of which waited for: 19 -> 18; matrix products, arithmetic and copies ran while one was open for 18% -> 12% of each run, Pallas kernels for 0% -> 0%
where the time goes in v1:
time: 209 us; the launch traced here: 208 us
  waiting for transfers between devices  82.6 us (40%)
  starting transfers between devices  40.4 us (19%)
  other arithmetic  29.9 us (14%)
  blocking collectives  21.5 us (10%)
  between operations  15.4 us (7%)
  local copies, waits for them, and re-layouts  12.2 us (6%)
  matrix products  6.15 us (3%)
    ppermute x10, waiting for transfers between devices, all_sum(): x = x + lax.ppermute(x, axis, [(i, i ^ step) for i in range(peers)])  24.2 us
    all_to_all x1, blocking collectives, on_device(): lax.all_to_all(own_columns, 'tensor', split_axis=0, concat_axis=1, tiled=...  21.5 us
    ppermute x5, waiting for transfers between devices, all_moments(): lax.ppermute(jnp.stack([mean, spread]), axis, [(i, i ^ step) for i in ran...  17.5 us
    all_gather x1, waiting for transfers between devices, gather_weight(): held = lax.all_gather(mine, 'tensor', axis=0, tiled=False)  15.7 us
    ppermute x3, waiting for transfers between devices, rows_sum(): x = keep + lax.ppermute(give, axis, [(i, i ^ step) for i in range(peers)])  10.2 us
    ppermute x2, starting transfers between devices, extended(): before = lax.ppermute(last, axis, up)  10.1 us
    ppermute x2, waiting for transfers between devices, on_device(): lax.ppermute(lower[-1] if lower else flat_grad, 'tensor', pairs)  9.31 us
    ppermute x5, starting transfers between devices, all_moments(): lax.ppermute(jnp.stack([mean, spread]), axis, [(i, i ^ step) for i in ran...  8.3 us
  transfers between devices with their start and end apart: 31, of which 18 were waited for; matrix products, arithmetic and copies ran while one was open for 12% of the time, Pallas kernels for 0%

profile of v1, /device:TPU:0, one launch (start us, length us, event | category | flops | bytes accessed | tf_op | source)
XLA Modules:
  0.0 208.1 jit_solution(18041520989941999849)
XLA Ops:
  7.2 1.4 fusion
  8.7 4.9 %collective-permute-start = (bf16[2,15,1536]{2,1,0:T(8,128)(2,1)S(1)}, bf16[2,15,1536]{2,1,0:T(8,128)(2,1)S(1)}, u32[]{:S(2)}, u32[]{:S(2)}) collective-permute-start(bf16[2,15,1536]{2,1,0:T(8,128)(2,1)S(1)} %get-tuple-element.99), channel_id=1, source_target_pairs={{0,1},{1,2},{2,3},{4,5},{5,6},{6,7},{8,9},{9,10},{10,11},{12,13},{... | collective-permute-start | bytes 276488 | tf_op jit(solution)/shard_map/ppermute | solution.py:22
  13.6 1.4 collective-permute-start.1
  15.9 4.4 %collective-permute-done.1 = bf16[2,15,1536]{2,1,0:T(8,128)(2,1)S(1)} collective-permute-done((bf16[2,15,1536]{2,1,0:T(8,128)(2,1)S(1)}, bf16[2,15,1536]{2,1,0:T(8,128)(2,1)S(1)}, u32[]{:S(2)}, u32[]{:S(2)}) %collective-permute-start.1) | collective-permute-done | bytes 92192 | tf_op jit(solution)/shard_map/ppermute | solution.py:23
  20.3 3.8 %fusion.145 = (f32[1536]{0:T(1024)S(1)}, f32[2,64,1536]{2,1,0:T(8,128)S(1)}) fusion(bf16[2,15,1536]{2,1,0:T(8,128)(2,1)S(1)} %collective-permute-done.1, bf16[2,64,1536]{2,1,0:T(8,128)(2,1)S(1)} %fusion, f32[1536]{0:T(1024)S(1)} %get-tuple-element.72, f32[1536]{0:T(1024)S(1)} %get-tuple-element.73, f32[1536]{0:T(1024)S(1)} %get-tuple-element.44, ...), kind=kLoop, calls=%fused_computation.389 | loop fusion | flops 35977728 | bytes 1560576 | tf_op jit(solution)/shard_map/reduce_sum | solution.py:127
  24.4 1.2 collective-permute-done.5
  25.6 1.6 collective-permute-start.6
  27.2 2.2 %collective-permute-done.6 = f32[2,1536]{1,0:T(2,128)S(1)} collective-permute-done((f32[2,1536]{1,0:T(2,128)S(1)}, f32[2,1536]{1,0:T(2,128)S(1)}, u32[]{:S(2)}, u32[]{:S(2)}) %collective-permute-start.6) | collective-permute-done | bytes 12320 | tf_op jit(solution)/shard_map/ppermute | solution.py:50
  29.4 1.6 collective-permute-start.7
  31.3 1.7 collective-permute-start.4
  33.5 1.6 collective-permute-start.8
  35.1 13.9 %collective-permute-done.8 = f32[2,1536]{1,0:T(2,128)S(1)} collective-permute-done((f32[2,1536]{1,0:T(2,128)S(1)}, f32[2,1536]{1,0:T(2,128)S(1)}, u32[]{:S(2)}, u32[]{:S(2)}) %collective-permute-start.8) | collective-permute-done | bytes 12320 | tf_op jit(solution)/shard_map/ppermute | solution.py:50
  49.1 3.4 %collective-permute-start.9 = (f32[2,1536]{1,0:T(2,128)S(1)}, f32[2,1536]{1,0:T(2,128)S(1)}, u32[]{:S(2)}, u32[]{:S(2)}) collective-permute-start(f32[2,1536]{1,0:T(2,128)S(1)} %pad_maximum_fusion.11), channel_id=1, source_target_pairs={{0,2},{1,3},{2,0},{3,1},{4,6},{5,7},{6,4},{7,5},{8,10},{9,11},{10,... | collective-permute-start | bytes 36872 | tf_op jit(solution)/shard_map/ppermute | solution.py:50
  52.5 1.4 collective-permute-start.3
  54.9 9.3 %collective-permute-done.3 = bf16[128,1536]{1,0:T(8,128)(2,1)S(1)} collective-permute-done((bf16[128,1536]{1,0:T(8,128)(2,1)}, bf16[128,1536]{1,0:T(8,128)(2,1)S(1)}, u32[]{:S(2)}, u32[]{:S(2)}) %collective-permute-start.3) | collective-permute-done | bytes 393248 | tf_op jit(solution)/shard_map/ppermute | solution.py:113
  64.2 2.3 %pad_maximum_fusion.1 = bf16[4,128,1536]{2,1,0:T(8,128)(2,1)} fusion(bf16[1,128,1536]{2,1,0:T(8,128)(2,1)S(1)} %bitcast.34, bf16[1,128,1536]{2,1,0:T(8,128)(2,1)S(1)} %bitcast.33, bf16[1,128,1536]{2,1,0:T(8,128)(2,1)} %bitcast.2, bf16[1,128,1536]{2,1,0:T(8,128)(2,1)S(1)} %bitcast.35), kind=kLoop, calls=%fused_computation.94 | loop fusion | flops 2359296 | bytes 3145728 | tf_op jit(solution)/shard_map/stack | solution.py:116
  66.5 3.2 %gather_fusion = bf16[4,128,1536]{2,1,0:T(8,128)(2,1)} fusion(bf16[4,128,1536]{2,1,0:T(8,128)(2,1)} %pad_maximum_fusion.1, s32[1024]{0:T(1024)S(1)} %pad_clamp_fusion), kind=kCustom, calls=%fused_computation | custom fusion | bytes 3145744 | tf_op jit(solution)/shard_map/gather | solution.py:118
  69.8 2.4 %fusion.149 = f32[512,384]{1,0:T(8,128)S(1)} fusion(bf16[512,1536]{1,0:T(8,128)(2,1)} %bitcast.24, bf16[384,1536]{1,0:T(8,128)(2,1)S(1)} %copy-done), kind=kOutput, calls=%fused_computation.392 | convolution fusion | flops 603979776 | bytes 3538944 | tf_op jit(solution)/shard_map/fd,cd->fc/dot_general | solution.py:138
  72.2 21.5 %all_to_all.35 = f32[4,128,384]{2,1,0:T(8,128)S(1)} all-to-all(f32[4,128,384]{2,1,0:T(8,128)S(1)} %bitcast.30), channel_id=1, replica_groups=mesh['dp'=8,'tensor'=4] {'tensor'}, dimensions={0} | all-to-all | bytes 1572864 | tf_op jit(solution)/shard_map/all_to_all | solution.py:141
  94.1 1.2 reshape.242
  95.3 2.5 %fusion.142 = (f32[1536]{0:T(1024)S(1)}, f32[1536]{0:T(1024)S(1)}, f32[2,64,1536]{2,1,0:T(8,128)}, bf16[2,64,1536]{2,1,0:T(8,128)(2,1)S(1)}) fusion(f32[1536]{0:T(1024)} %get-tuple-element.90, f32[2,64,1536]{2,1,0:T(8,128)S(1)} %get-tuple-element.93, f32[1536]{0:T(1024)} %get-tuple-element.8, f32[2,64,1536]{2,1,0:T(8,128)} %reshape.242, f32[1536]{0:T(1024)} %param.9, ...), kind=kLoop, calls=%fused_computation.387 | loop fusion | flops 3142656 | bytes 2789376 | tf_op jit(solution)/shard_map/reduce_sum | solution.py:154
  98.1 3.5 %collective-permute-done.11 = f32[2,1536]{1,0:T(2,128)S(1)} collective-permute-done((f32[2,1536]{1,0:T(2,128)S(1)}, f32[2,1536]{1,0:T(2,128)S(1)}, u32[]{:S(2)}, u32[]{:S(2)}) %collective-permute-start.11) | collective-permute-done | bytes 12320 | tf_op jit(solution)/shard_map/ppermute | solution.py:40
  102.8 4.0 %all-to-all-start.1 = ((bf16[128,4,384]{2,0,1:T(8,128)(2,1)}), bf16[128,4,384]{2,0,1:T(8,128)(2,1)S(1)}, u32[]{:S(2)}, u32[]{:S(2)}) async-start(bf16[128,4,384]{2,0,1:T(8,128)(2,1)} %copy.17), calls=%async_computation.1 | async-start | bytes 786432 | tf_op jit(solution)/shard_map/all_to_all | solution.py:150
  106.9 1.2 collective-permute-done.13
  108.1 1.6 collective-permute-start.14
  109.6 2.2 %collective-permute-done.14 = f32[2,1536]{1,0:T(2,128)S(1)} collective-permute-done((f32[2,1536]{1,0:T(2,128)S(1)}, f32[2,1536]{1,0:T(2,128)S(1)}, u32[]{:S(2)}, u32[]{:S(2)}) %collective-permute-start.14) | collective-permute-done | bytes 12320 | tf_op jit(solution)/shard_map/ppermute | solution.py:40
  113.3 2.3 %collective-permute-done.15 = f32[2,1536]{1,0:T(2,128)S(1)} collective-permute-done((f32[2,1536]{1,0:T(2,128)S(1)}, f32[2,1536]{1,0:T(2,128)S(1)}, u32[]{:S(2)}, u32[]{:S(2)}) %collective-permute-start.15) | collective-permute-done | bytes 12320 | tf_op jit(solution)/shard_map/ppermute | solution.py:40
  115.9 2.2 %fusion.150 = f32[384,1536]{1,0:T(8,128)S(1)} fusion(bf16[512,384]{1,0:T(8,128)(2,1)S(1)} %bitcast.29, bf16[512,1536]{1,0:T(8,128)(2,1)} %bitcast.25), kind=kOutput, calls=%fused_computation.393 | convolution fusion | flops 603979776 | bytes 4325376 | tf_op jit(solution)/shard_map/fc,fd->cd/dot_general | solution.py:151
  119.2 1.6 fusion.80
  120.8 1.2 fusion.64
  122.2 1.0 copy-done.2
  123.2 1.6 collective-permute-start.19
  127.3 1.4 collective-permute-done.24
  129.3 10.2 %collective-permute-done.19 = f32[96,1536]{1,0:T(8,128)} collective-permute-done((f32[96,1536]{1,0:T(8,128)S(1)}, f32[96,1536]{1,0:T(8,128)}, u32[]{:S(2)}, u32[]{:S(2)}) %collective-permute-start.19) | collective-permute-done | bytes 589856 | tf_op jit(solution)/shard_map/ppermute | solution.py:73
  139.5 1.3 dynamic-slice_add_fusion.1
  143.6 1.3 collective-permute-start.16
  144.9 5.2 %collective-permute-start.17 = (bf16[2,15,1536]{2,1,0:T(8,128)(2,1)}, bf16[2,15,1536]{2,1,0:T(8,128)(2,1)}, u32[]{:S(2)}, u32[]{:S(2)}) collective-permute-start(bf16[2,15,1536]{2,1,0:T(8,128)(2,1)} %get-tuple-element.98), channel_id=1, source_target_pairs={{0,1},{1,2},{2,3},{4,5},{5,6},{6,7},{8,9},{9,10},{10,11},{12,13},{... | collective-permute-start | bytes 276488 | tf_op jit(solution)/shard_map/ppermute | solution.py:22
  150.1 1.6 collective-permute-start.26
  151.7 15.7 %all-gather.3.cloned.1.call-done = bf16[768,1536]{1,0:T(8,128)(2,1)} async-done(((bf16[192,1536]{1,0:T(8,128)(2,1)}), bf16[768,1536]{1,0:T(8,128)(2,1)}) %all-gather.3.cloned.1.call-update) | async-done | bytes 2359312 | tf_op jit(solution)/shard_map/all_gather | solution.py:89
  167.4 1.1 dynamic-slice_add_fusion.2
  168.5 1.5 collective-permute-start.21
  170.0 7.4 %multiply_convert_fusion = (bf16[2,64,1536]{2,1,0:T(8,128)(2,1)S(1)}, f32[2,64,1536]{2,1,0:T(8,128)S(1)}) fusion(bf16[2,64,3072]{2,1,0:T(8,128)(2,1)S(1)} %copy-done.1, bf16[2,64,1536]{2,1,0:T(8,128)(2,1)S(1)} %get-tuple-element.86, bf16[2,15,1536]{2,1,0:T(8,128)(2,1)} %collective-permute-done.17, f32[1536]{0:T(1024)} %copy-done.41, f32[1536]{0:T(1024)} %copy-done.42, ...), kind=kLoop, calls=%fused_computation.212 | loop fusion | flops 36962304 | bytes 2340864 | tf_op jit(solution)/shard_map/convert
  178.0 1.5 collective-permute-start.22
  179.8 4.7 %collective-permute-done.27 = f32[31,1536]{1,0:T(8,128)S(1)} collective-permute-done((f32[31,1536]{1,0:T(8,128)S(1)}, f32[31,1536]{1,0:T(8,128)S(1)}, u32[]{:S(2)}, u32[]{:S(2)}) %collective-permute-start.27) | collective-permute-done | bytes 190496 | tf_op jit(solution)/shard_map/ppermute | solution.py:40
  184.6 1.4 collective-permute-start.28
  186.9 9.0 %collective-permute-done.28 = f32[31,1536]{1,0:T(8,128)S(1)} collective-permute-done((f32[31,1536]{1,0:T(8,128)S(1)}, f32[31,1536]{1,0:T(8,128)S(1)}, u32[]{:S(2)}, u32[]{:S(2)}) %collective-permute-start.28) | collective-permute-done | bytes 190496 | tf_op jit(solution)/shard_map/ppermute | solution.py:40
  197.5 1.5 convolution_convert_fusion
  199.7 1.6 maximum_select_fusion
  (209 shorter events, 17.0 us)
Async XLA Ops:
  7.2 62.6 %copy-start = (bf16[384,1536]{1,0:T(8,128)(2,1)S(1)}, bf16[384,1536]{1,0:T(8,128)(2,1)}, u32[]{:S(2)}) copy-start(bf16[384,1536]{1,0:T(8,128)(2,1)} %param.10) | copy-start | bytes 3538948
  8.7 7.2 %collective-permute-start = (bf16[2,15,1536]{2,1,0:T(8,128)(2,1)S(1)}, bf16[2,15,1536]{2,1,0:T(8,128)(2,1)S(1)}, u32[]{:S(2)}, u32[]{:S(2)}) collective-permute-start(bf16[2,15,1536]{2,1,0:T(8,128)(2,1)S(1)} %get-tuple-element.99), channel_id=1, source_target_pairs={{0,1},{1,2},{2,3},{4,5},{5,6},{6,7},{8,9},{9,10},{10,11},{12,13},{... | collective-permute-start | bytes 276488 | tf_op jit(solution)/shard_map/ppermute | solution.py:22
  13.6 17.7 %copy-start.10 = (bf16[2,64,1536]{2,1,0:T(8,128)(2,1)S(1)}, bf16[2,64,1536]{2,1,0:T(8,128)(2,1)}, u32[]{:S(2)}) copy-start(bf16[2,64,1536]{2,1,0:T(8,128)(2,1)} %param.11) | copy-start | bytes 1179652
  13.6 6.6 %collective-permute-start.1 = (bf16[2,15,1536]{2,1,0:T(8,128)(2,1)S(1)}, bf16[2,15,1536]{2,1,0:T(8,128)(2,1)S(1)}, u32[]{:S(2)}, u32[]{:S(2)}) collective-permute-start(bf16[2,15,1536]{2,1,0:T(8,128)(2,1)S(1)} %get-tuple-element.100), channel_id=1, source_target_pairs={{1,0},{2,1},{3,2},{5,4},{6,5},{7,6},{9,8},{10,9},{11,10},{13,12},{... | collective-permute-start | bytes 276488 | tf_op jit(solution)/shard_map/ppermute | solution.py:23
  15.4 15.6 %copy-start.12 = (f32[1536]{0:T(1024)}, f32[1536]{0:T(1024)S(1)}, u32[]{:S(2)}) copy-start(f32[1536]{0:T(1024)S(1)} %get-tuple-element.45) | copy-start | bytes 18436
  15.4 15.6 %copy-start.13 = (f32[1536]{0:T(1024)}, f32[1536]{0:T(1024)S(1)}, u32[]{:S(2)}) copy-start(f32[1536]{0:T(1024)S(1)} %get-tuple-element.46) | copy-start | bytes 18436
  15.4 15.6 %copy-start.14 = (f32[1536]{0:T(1024)}, f32[1536]{0:T(1024)S(1)}, u32[]{:S(2)}) copy-start(f32[1536]{0:T(1024)S(1)} %get-tuple-element.47) | copy-start | bytes 18436
  15.4 15.6 %copy-start.15 = (f32[1536]{0:T(1024)}, f32[1536]{0:T(1024)S(1)}, u32[]{:S(2)}) copy-start(f32[1536]{0:T(1024)S(1)} %get-tuple-element.48) | copy-start | bytes 18436
  15.4 15.6 %copy-start.16 = (f32[1536]{0:T(1024)}, f32[1536]{0:T(1024)S(1)}, u32[]{:S(2)}) copy-start(f32[1536]{0:T(1024)S(1)} %get-tuple-element.49) | copy-start | bytes 18436
  15.4 15.6 %copy-start.17 = (f32[1536]{0:T(1024)}, f32[1536]{0:T(1024)S(1)}, u32[]{:S(2)}) copy-start(f32[1536]{0:T(1024)S(1)} %get-tuple-element.50) | copy-start | bytes 18436
  15.5 15.6 %copy-start.18 = (f32[1536]{0:T(1024)}, f32[1536]{0:T(1024)S(1)}, u32[]{:S(2)}) copy-start(f32[1536]{0:T(1024)S(1)} %get-tuple-element.51) | copy-start | bytes 18436
  15.5 15.6 %copy-start.19 = (f32[1536]{0:T(1024)}, f32[1536]{0:T(1024)S(1)}, u32[]{:S(2)}) copy-start(f32[1536]{0:T(1024)S(1)} %get-tuple-element.52) | copy-start | bytes 18436
  15.5 15.6 %copy-start.20 = (f32[1536]{0:T(1024)}, f32[1536]{0:T(1024)S(1)}, u32[]{:S(2)}) copy-start(f32[1536]{0:T(1024)S(1)} %get-tuple-element.53) | copy-start | bytes 18436
  15.5 15.6 %copy-start.21 = (f32[1536]{0:T(1024)}, f32[1536]{0:T(1024)S(1)}, u32[]{:S(2)}) copy-start(f32[1536]{0:T(1024)S(1)} %get-tuple-element.54) | copy-start | bytes 18436
  15.5 15.6 %copy-start.22 = (f32[1536]{0:T(1024)}, f32[1536]{0:T(1024)S(1)}, u32[]{:S(2)}) copy-start(f32[1536]{0:T(1024)S(1)} %get-tuple-element.55) | copy-start | bytes 18436
  15.9 38.3 %copy-start.43 = (f32[1536]{0:T(1024)S(1)}, f32[1536]{0:T(1024)}, u32[]{:S(2)}) copy-start(f32[1536]{0:T(1024)} %param.8) | copy-start | bytes 18436
  15.9 50.6 %copy-start.8 = (bf16[2,15,1536]{2,1,0:T(8,128)(2,1)}, bf16[2,15,1536]{2,1,0:T(8,128)(2,1)S(1)}, u32[]{:S(2)}) copy-start(bf16[2,15,1536]{2,1,0:T(8,128)(2,1)S(1)} %collective-permute-done) | copy-start | bytes 276484
  20.3 46.3 %copy-start.6 = (bf16[2,15,1536]{2,1,0:T(8,128)(2,1)}, bf16[2,15,1536]{2,1,0:T(8,128)(2,1)S(1)}, u32[]{:S(2)}) copy-start(bf16[2,15,1536]{2,1,0:T(8,128)(2,1)S(1)} %collective-permute-done.1) | copy-start | bytes 276484
  24.3 1.2 collective-permute-start.5
  25.6 3.8 %collective-permute-start.6 = (f32[2,1536]{1,0:T(2,128)S(1)}, f32[2,1536]{1,0:T(2,128)S(1)}, u32[]{:S(2)}, u32[]{:S(2)}) collective-permute-start(f32[2,1536]{1,0:T(2,128)S(1)} %pad_maximum_fusion.8), channel_id=1, source_target_pairs={{0,8},{4,12},{8,0},{12,4},{16,24},{20,28},{24,16},{28,20},{1,9},{5... | collective-permute-start | bytes 36872 | tf_op jit(solution)/shard_map/ppermute | solution.py:50
  29.4 3.9 %collective-permute-start.7 = (f32[2,1536]{1,0:T(2,128)S(1)}, f32[2,1536]{1,0:T(2,128)S(1)}, u32[]{:S(2)}, u32[]{:S(2)}) collective-permute-start(f32[2,1536]{1,0:T(2,128)S(1)} %pad_maximum_fusion.9), channel_id=1, source_target_pairs={{0,16},{4,20},{8,24},{12,28},{16,0},{20,4},{24,8},{28,12},{1,17},{... | collective-permute-start | bytes 36872 | tf_op jit(solution)/shard_map/ppermute | solution.py:50
  31.3 23.6 %collective-permute-start.4 = (bf16[128,1536]{1,0:T(8,128)(2,1)S(1)}, bf16[128,1536]{1,0:T(8,128)(2,1)S(1)}, u32[]{:S(2)}, u32[]{:S(2)}) collective-permute-start(bf16[128,1536]{1,0:T(8,128)(2,1)S(1)} %bitcast.31), channel_id=1, source_target_pairs={{1,0},{2,1},{3,2},{0,3},{5,4},{6,5},{7,6},{4,7},{9,8},{10,9},{11,1... | collective-permute-start | bytes 1179656 | tf_op jit(solution)/shard_map/ppermute | solution.py:115
  33.0 19.5 %collective-permute-start.2 = (bf16[128,1536]{1,0:T(8,128)(2,1)S(1)}, bf16[128,1536]{1,0:T(8,128)(2,1)}, u32[]{:S(2)}, u32[]{:S(2)}) collective-permute-start(bf16[128,1536]{1,0:T(8,128)(2,1)S(1)} %bitcast.32), channel_id=1, source_target_pairs={{0,1},{1,2},{2,3},{3,0},{4,5},{5,6},{6,7},{7,4},{8,9},{9,10},{10,1... | collective-permute-start | bytes 1179656 | tf_op jit(solution)/shard_map/ppermute | solution.py:113
  33.5 15.6 %collective-permute-start.8 = (f32[2,1536]{1,0:T(2,128)S(1)}, f32[2,1536]{1,0:T(2,128)S(1)}, u32[]{:S(2)}, u32[]{:S(2)}) collective-permute-start(f32[2,1536]{1,0:T(2,128)S(1)} %pad_maximum_fusion.10), channel_id=1, source_target_pairs={{0,1},{1,0},{2,3},{3,2},{4,5},{5,4},{6,7},{7,6},{8,9},{9,8},{10,11... | collective-permute-start | bytes 36872 | tf_op jit(solution)/shard_map/ppermute | solution.py:50
  49.1 5.1 %collective-permute-start.9 = (f32[2,1536]{1,0:T(2,128)S(1)}, f32[2,1536]{1,0:T(2,128)S(1)}, u32[]{:S(2)}, u32[]{:S(2)}) collective-permute-start(f32[2,1536]{1,0:T(2,128)S(1)} %pad_maximum_fusion.11), channel_id=1, source_target_pairs={{0,2},{1,3},{2,0},{3,1},{4,6},{5,7},{6,4},{7,5},{8,10},{9,11},{10,... | collective-permute-start | bytes 36872 | tf_op jit(solution)/shard_map/ppermute | solution.py:50
  52.5 11.7 %collective-permute-start.3 = (bf16[128,1536]{1,0:T(8,128)(2,1)}, bf16[128,1536]{1,0:T(8,128)(2,1)S(1)}, u32[]{:S(2)}, u32[]{:S(2)}) collective-permute-start(bf16[128,1536]{1,0:T(8,128)(2,1)} %collective-permute-done.2), channel_id=1, source_target_pairs={{0,1},{1,2},{2,3},{3,0},{4,5},{5,6},{6,7},{7,4},{8,9},{9,10},{10,1... | collective-permute-start | bytes 1179656 | tf_op jit(solution)/shard_map/ppermute | solution.py:113
  97.9 3.8 %collective-permute-start.11 = (f32[2,1536]{1,0:T(2,128)S(1)}, f32[2,1536]{1,0:T(2,128)S(1)}, u32[]{:S(2)}, u32[]{:S(2)}) collective-permute-start(f32[2,1536]{1,0:T(2,128)S(1)} %pad_maximum_fusion.12), channel_id=1, source_target_pairs={{0,1},{1,0},{2,3},{3,2},{4,5},{5,4},{6,7},{7,6},{8,9},{9,8},{10,11... | collective-permute-start | bytes 36872 | tf_op jit(solution)/shard_map/ppermute | solution.py:40
  101.6 5.2 %collective-permute-start.12 = (f32[2,1536]{1,0:T(2,128)S(1)}, f32[2,1536]{1,0:T(2,128)S(1)}, u32[]{:S(2)}, u32[]{:S(2)}) collective-permute-start(f32[2,1536]{1,0:T(2,128)S(1)} %fusion.141), channel_id=1, source_target_pairs={{0,2},{1,3},{2,0},{3,1},{4,6},{5,7},{6,4},{7,5},{8,10},{9,11},{10,... | collective-permute-start | bytes 36872 | tf_op jit(solution)/shard_map/ppermute | solution.py:40
  102.8 13.0 %all-to-all-start.1 = ((bf16[128,4,384]{2,0,1:T(8,128)(2,1)}), bf16[128,4,384]{2,0,1:T(8,128)(2,1)S(1)}, u32[]{:S(2)}, u32[]{:S(2)}) async-start(bf16[128,4,384]{2,0,1:T(8,128)(2,1)} %copy.17), calls=%async_computation.1 | async-start | bytes 786432 | tf_op jit(solution)/shard_map/all_to_all | solution.py:150
  106.8 60.6 %all-gather.3.cloned.1.call-start = ((), (), s32[]{:S(2)}) async-start(), calls=%async_computation.2 | async-start | bytes 2949120 | tf_op jit(solution)/shard_map/all_gather | solution.py:89
  106.8 1.2 collective-permute-start.13
  108.1 3.8 %collective-permute-start.14 = (f32[2,1536]{1,0:T(2,128)S(1)}, f32[2,1536]{1,0:T(2,128)S(1)}, u32[]{:S(2)}, u32[]{:S(2)}) collective-permute-start(f32[2,1536]{1,0:T(2,128)S(1)} %add.522), channel_id=1, source_target_pairs={{0,8},{4,12},{8,0},{12,4},{16,24},{20,28},{24,16},{28,20},{1,9},{5... | collective-permute-start | bytes 36872 | tf_op jit(solution)/shard_map/ppermute | solution.py:40
  111.9 3.8 %collective-permute-start.15 = (f32[2,1536]{1,0:T(2,128)S(1)}, f32[2,1536]{1,0:T(2,128)S(1)}, u32[]{:S(2)}, u32[]{:S(2)}) collective-permute-start(f32[2,1536]{1,0:T(2,128)S(1)} %add.523), channel_id=1, source_target_pairs={{0,16},{4,20},{8,24},{12,28},{16,0},{20,4},{24,8},{28,12},{1,17},{... | collective-permute-start | bytes 36872 | tf_op jit(solution)/shard_map/ppermute | solution.py:40
  118.2 3.8 %collective-permute-start.18 = (f32[192,1536]{1,0:T(8,128)S(1)}, f32[192,1536]{1,0:T(8,128)S(1)}, u32[]{:S(2)}, u32[]{:S(2)}) collective-permute-start(f32[192,1536]{1,0:T(8,128)S(1)} %constant_dynamic-slice_fusion.2), channel_id=1, source_target_pairs={{0,4},{4,0},{8,12},{12,8},{16,20},{20,16},{24,28},{28,24},{1,5},{5... | collective-permute-start | bytes 3538952 | tf_op jit(solution)/shard_map/ppermute | solution.py:73
  123.2 16.3 %collective-permute-start.19 = (f32[96,1536]{1,0:T(8,128)S(1)}, f32[96,1536]{1,0:T(8,128)}, u32[]{:S(2)}, u32[]{:S(2)}) collective-permute-start(f32[96,1536]{1,0:T(8,128)S(1)} %constant_dynamic-slice_fusion.1), channel_id=1, source_target_pairs={{0,8},{4,12},{8,0},{12,4},{16,24},{20,28},{24,16},{28,20},{1,9},{5... | collective-permute-start | bytes 1769480 | tf_op jit(solution)/shard_map/ppermute | solution.py:73
  127.2 1.5 collective-permute-start.24
  128.7 21.4 %collective-permute-start.25 = (f32[31,1536]{1,0:T(8,128)S(1)}, f32[31,1536]{1,0:T(8,128)S(1)}, u32[]{:S(2)}, u32[]{:S(2)}) collective-permute-start(f32[31,1536]{1,0:T(8,128)S(1)} %add.563), channel_id=1, source_target_pairs={{0,8},{4,12},{8,0},{12,4},{16,24},{20,28},{24,16},{28,20},{1,9},{5... | collective-permute-start | bytes 571400 | tf_op jit(solution)/shard_map/ppermute | solution.py:40
  141.7 28.3 %copy-start.1 = (bf16[2,64,3072]{2,1,0:T(8,128)(2,1)S(1)}, bf16[2,64,3072]{2,1,0:T(8,128)(2,1)}, u32[]{:S(2)}) copy-start(bf16[2,64,3072]{2,1,0:T(8,128)(2,1)} %param.6) | copy-start | bytes 2359300
  142.4 25.0 %collective-permute-start.20 = (f32[48,1536]{1,0:T(8,128)}, f32[48,1536]{1,0:T(8,128)}, u32[]{:S(2)}, u32[]{:S(2)}) collective-permute-start(f32[48,1536]{1,0:T(8,128)} %constant_dynamic-slice_fusion), channel_id=1, source_target_pairs={{0,16},{4,20},{8,24},{12,28},{16,0},{20,4},{24,8},{28,12},{1,17},{... | collective-permute-start | bytes 884744 | tf_op jit(solution)/shard_map/ppermute | solution.py:73
  143.6 26.4 %collective-permute-start.16 = (bf16[2,15,1536]{2,1,0:T(8,128)(2,1)}, bf16[2,15,1536]{2,1,0:T(8,128)(2,1)}, u32[]{:S(2)}, u32[]{:S(2)}) collective-permute-start(bf16[2,15,1536]{2,1,0:T(8,128)(2,1)} %get-tuple-element.97), channel_id=1, source_target_pairs={{1,0},{2,1},{3,2},{5,4},{6,5},{7,6},{9,8},{10,9},{11,10},{13,12},{... | collective-permute-start | bytes 276488 | tf_op jit(solution)/shard_map/ppermute | solution.py:23
  144.9 25.1 %collective-permute-start.17 = (bf16[2,15,1536]{2,1,0:T(8,128)(2,1)}, bf16[2,15,1536]{2,1,0:T(8,128)(2,1)}, u32[]{:S(2)}, u32[]{:S(2)}) collective-permute-start(bf16[2,15,1536]{2,1,0:T(8,128)(2,1)} %get-tuple-element.98), channel_id=1, source_target_pairs={{0,1},{1,2},{2,3},{4,5},{5,6},{6,7},{8,9},{9,10},{10,11},{12,13},{... | collective-permute-start | bytes 276488 | tf_op jit(solution)/shard_map/ppermute | solution.py:22
  150.1 27.3 %collective-permute-start.26 = (f32[31,1536]{1,0:T(8,128)S(1)}, f32[31,1536]{1,0:T(8,128)S(1)}, u32[]{:S(2)}, u32[]{:S(2)}) collective-permute-start(f32[31,1536]{1,0:T(8,128)S(1)} %add.564), channel_id=1, source_target_pairs={{0,16},{4,20},{8,24},{12,28},{16,0},{20,4},{24,8},{28,12},{1,17},{... | collective-permute-start | bytes 571400 | tf_op jit(solution)/shard_map/ppermute | solution.py:40
  167.4 29.5 %collective-permute-start.10 = (bf16[4,192,1536]{2,1,0:T(8,128)(2,1)}, bf16[4,192,1536]{2,1,0:T(8,128)(2,1)S(1)}, u32[]{:S(2)}, u32[]{:S(2)}) collective-permute-start(bf16[4,192,1536]{2,1,0:T(8,128)(2,1)} %bitcast.27), channel_id=1, source_target_pairs={{0,4},{4,0},{8,12},{12,8},{16,20},{20,16},{24,28},{28,24},{1,5},{5... | collective-permute-start | bytes 7077896 | tf_op jit(solution)/shard_map/ppermute | solution.py:90
  168.5 9.5 %collective-permute-start.21 = (f32[48,1536]{1,0:T(8,128)S(1)}, f32[48,1536]{1,0:T(8,128)S(1)}, u32[]{:S(2)}, u32[]{:S(2)}) collective-permute-start(f32[48,1536]{1,0:T(8,128)S(1)} %dynamic-slice_add_fusion.2), channel_id=1, source_target_pairs={{0,16},{4,20},{8,24},{12,28},{16,0},{20,4},{24,8},{28,12},{1,17},{... | collective-permute-start | bytes 884744 | tf_op jit(solution)/shard_map/ppermute | solution.py:77
  177.4 7.1 %collective-permute-start.27 = (f32[31,1536]{1,0:T(8,128)S(1)}, f32[31,1536]{1,0:T(8,128)S(1)}, u32[]{:S(2)}, u32[]{:S(2)}) collective-permute-start(f32[31,1536]{1,0:T(8,128)S(1)} %add.565), channel_id=1, source_target_pairs={{0,1},{1,0},{2,3},{3,2},{4,5},{5,4},{6,7},{7,6},{8,9},{9,8},{10,11... | collective-permute-start | bytes 571400 | tf_op jit(solution)/shard_map/ppermute | solution.py:40
  178.0 18.7 %collective-permute-start.22 = (f32[96,1536]{1,0:T(8,128)S(1)}, f32[96,1536]{1,0:T(8,128)S(1)}, u32[]{:S(2)}, u32[]{:S(2)}) collective-permute-start(f32[96,1536]{1,0:T(8,128)S(1)} %maximum_select_fusion.2), channel_id=1, source_target_pairs={{0,8},{4,12},{8,0},{12,4},{16,24},{20,28},{24,16},{28,20},{1,9},{5... | collective-permute-start | bytes 1769480 | tf_op jit(solution)/shard_map/ppermute | solution.py:77
  184.6 11.4 %collective-permute-start.28 = (f32[31,1536]{1,0:T(8,128)S(1)}, f32[31,1536]{1,0:T(8,128)S(1)}, u32[]{:S(2)}, u32[]{:S(2)}) collective-permute-start(f32[31,1536]{1,0:T(8,128)S(1)} %add.566), channel_id=1, source_target_pairs={{0,2},{1,3},{2,0},{3,1},{4,6},{5,7},{6,4},{7,5},{8,10},{9,11},{10,... | collective-permute-start | bytes 571400 | tf_op jit(solution)/shard_map/ppermute | solution.py:40
  196.7 2.9 %collective-permute-start.23 = (f32[192,1536]{1,0:T(8,128)S(1)}, f32[192,1536]{1,0:T(8,128)S(1)}, u32[]{:S(2)}, u32[]{:S(2)}) collective-permute-start(f32[192,1536]{1,0:T(8,128)S(1)} %maximum_select_fusion.1), channel_id=1, source_target_pairs={{0,4},{4,0},{8,12},{12,8},{16,20},{20,16},{24,28},{28,24},{1,5},{5... | collective-permute-start | bytes 3538952 | tf_op jit(solution)/shard_map/ppermute | solution.py:77
  (30 other events, 310.5 us)
Sparse Core Ops, SparseCore 0:
  113.4 53.8 all-gather.2
